TPU v7x, 512 devices: a whole 4x8x8 slice. The times are simulated.
512 devices in a mesh: member: 16 (over x_lo, y), dp: 32 (over z, x_hi, core).
Axes of the slice: x: 4 (x_hi: 2, x_lo: 2; x = x_hi * 2 + x_lo), y: 8, z: 8, core: 2. Of those that a mesh axis runs over, the one named last changes fastest.
Arguments:
- inputs: bfloat16 [8192, 64], P('dp'), may hold values from -6 to 6
- observed: float32 [64, 8192], P('member', 'dp'), may hold values from -6 to 6
- noise: bfloat16 [2, 32, 64, 8192], P(None, None, 'member', 'dp'), may hold values from -4 to 4
- w_in: float32 [32, 64, 4096], P('member', None, 'dp'), may hold values from -0.75 to 0.75
- b_in: float32 [32, 4096], P('member', 'dp'), may hold values from -3 to 3
- w_out: float32 [32, 64, 4096], P('member', None, 'dp'), may hold values from -0.09375 to 0.09375
- b_out: float32 [32, 64], P('member'), may hold values from -3 to 3
Outputs:
- new_w_in: float32 [32, 64, 4096], P('member', None, 'dp')
- new_b_in: float32 [32, 4096], P('member', 'dp')
- new_w_out: float32 [32, 64, 4096], P('member', None, 'dp')
- new_b_out: float32 [32, 64], P('member')
All inputs are finite; a program needn't handle non-finite values.
Results may differ from a plain program's by a relative error of at most 0.00056.
Values may be sent and summed in bfloat16 or wider, within the bound.
No kernel may reach another device: no remote copies, remote signals or barrier semaphores. Data moves between devices by JAX's collectives and lax.ppermute only.
A program may use at most 64 MiB of HBM per device.

v0:
```python
import jax
import jax.numpy as jnp
from jax import lax
from jax.sharding import PartitionSpec as P

UPDATES = 2
ridge_level = 0.5


def solve_gain(gram, cross):
    eye = jnp.eye(gram.shape[0], dtype=gram.dtype)
    factor = jnp.linalg.cholesky(gram + ridge_level * eye)
    middle = lax.linalg.triangular_solve(factor, cross, left_side=True, lower=True)
    return lax.linalg.triangular_solve(factor, middle, left_side=True, lower=True, transpose_a=True)


def predict(inputs, w_in, b_in, w_out, b_out):
    shards = (
        w_in.astype(jnp.bfloat16),
        w_out.astype(jnp.bfloat16),
        b_in.astype(jnp.bfloat16)[:, None, :],
    )

    def single(item):
        weight_in, weight_out, bias_in = item
        pre = jnp.dot(inputs, weight_in, preferred_element_type=jnp.float32) + bias_in.astype(
            jnp.float32
        )
        hidden = jnp.tanh(pre).astype(jnp.bfloat16)
        return lax.dot_general(
            weight_out, hidden, (((1,), (1,)), ((), ())), preferred_element_type=jnp.float32
        )

    total = lax.map(
        single,
        (
            lax.all_gather(shards[0], "dp", axis=2, tiled=True),
            lax.all_gather(shards[1], "dp", axis=2, tiled=True),
            lax.all_gather(shards[2], "dp", axis=2, tiled=True),
        ),
    )
    return total + b_out[:, :, None]


def mix_own(own, whole, columns):
    flat = whole.reshape(whole.shape[0], -1)
    moved = lax.dot_general(
        columns, flat, (((0,), (0,)), ((), ())), precision=lax.Precision.HIGHEST
    )
    return own + moved.reshape(own.shape)


def on_device(inputs, observed, noise, w_in, b_in, w_out, b_out):
    per_device = w_in.shape[0]
    count = observed.shape[0] * lax.axis_size("member") * observed.shape[1] * lax.axis_size("dp")
    for update in range(UPDATES):
        predicted = predict(inputs, w_in, b_in, w_out, b_out)
        collected = lax.all_to_all(
            predicted.astype(jnp.bfloat16), "member", split_axis=1, concat_axis=0, tiled=True
        ).astype(predicted.dtype)
        mean_pred = jnp.mean(collected, axis=0)
        anomaly = (collected - mean_pred[None]).reshape(collected.shape[0], -1)
        misfit = (observed[None] + noise[update].astype(jnp.float32) - collected).reshape(
            collected.shape[0], -1
        )
        gram_part = lax.dot_general(
            anomaly, anomaly, (((1,), (1,)), ((), ())), precision=lax.Precision.HIGHEST
        )
        cross_part = lax.dot_general(
            anomaly, misfit, (((1,), (1,)), ((), ())), precision=lax.Precision.HIGHEST
        )
        gram, cross = lax.psum((gram_part, cross_part), ("member", "dp"))
        gain = solve_gain(gram / count, cross / count)
        whole_in, whole_bias, whole_out, whole_bout = (
            lax.all_gather(w_in, "member", axis=0, tiled=True),
            lax.all_gather(b_in, "member", axis=0, tiled=True),
            lax.all_gather(w_out, "member", axis=0, tiled=True),
            lax.all_gather(b_out, "member", axis=0, tiled=True),
        )
        first = lax.axis_index("member") * per_device
        columns = lax.dynamic_slice_in_dim(gain, first, per_device, 1)
        w_in = mix_own(w_in, whole_in, columns)
        b_in = mix_own(b_in, whole_bias, columns)
        w_out = mix_own(w_out, whole_out, columns)
        b_out = mix_own(b_out, whole_bout, columns)
    return (w_in, b_in, w_out, b_out)


def solution(mesh):
    placed = (
        P("dp", None),
        P("member", "dp"),
        P(None, None, "member", "dp"),
        P("member", None, "dp"),
        P("member", "dp"),
        P("member", None, "dp"),
        P("member", None),
    )
    return jax.shard_map(
        on_device,
        mesh=mesh,
        in_specs=placed,
        out_specs=(
            P("member", None, "dp"),
            P("member", "dp"),
            P("member", None, "dp"),
            P("member", None),
        ),
        check_vma=False,
    )
```

profile of v0, /device:TPU:1, one launch (start us, length us, event | category | flops | bytes accessed | tf_op | source)
XLA Modules:
  0.0 656.1 jit_solution(13720734547421046891)
XLA Ops:
  7.2 1.5 convert_element_type.118
  8.7 1.5 convert_element_type.119
  10.3 0.7 all-gather.21.cloned.1.call-update
  11.0 0.7 convert_element_type.120
  11.7 48.9 %all-gather = bf16[2,4096]{1,0:T(2,128)(2,1)S(1)} all-gather(bf16[2,128]{1,0:T(2,128)(2,1)S(1)} %convert_element_type.120), channel_id=2, replica_groups=mesh['member'=16,'dp'=32] {'dp'}, dimensions={1}, use_global_device_ids=true | all-gather | bytes 16896 | tf_op jit(solution)/shard_map/all_gather | solution.py:39
  60.6 35.2 %all-gather.15.cloned.1.call-done = bf16[2,64,4096]{2,1,0:T(8,128)(2,1)} async-done(((bf16[2,64,128]{2,1,0:T(8,128)(2,1)}), bf16[2,64,4096]{2,1,0:T(8,128)(2,1)}) %all-gather.15.cloned.1.call-update) | async-done | bytes 1048592 | tf_op jit(solution)/shard_map/all_gather | solution.py:38
  95.8 79.4 %all-gather.17.cloned.1.call-done = bf16[2,64,4096]{2,1,0:T(8,128)(2,1)} async-done(((bf16[2,64,128]{2,1,0:T(8,128)(2,1)}), bf16[2,64,4096]{2,1,0:T(8,128)(2,1)}) %all-gather.17.cloned.1.call-update) | async-done | bytes 1048592 | tf_op jit(solution)/shard_map/all_gather | solution.py:37
  175.2 5.3 while.20
  175.3 2.6 fusion.92
  177.9 2.6 fusion.92
  180.6 0.7 copy.79
  181.3 6.6 %all-to-all-start = ((bf16[2,64,256]{2,0,1:T(2,128)(2,1)}), bf16[2,64,256]{2,0,1:T(2,128)(2,1)S(1)}, u32[]{:S(2)}, u32[]{:S(2)}) async-start(bf16[2,64,256]{2,0,1:T(2,128)(2,1)} %copy.79), calls=%async_computation | async-start | bytes 131072 | tf_op jit(solution)/shard_map/all_to_all | solution.py:58
  188.0 0.5 all-gather.19.cloned.1.call-update
  188.5 6.8 %all-to-all-done = bf16[2,64,256]{2,0,1:T(2,128)(2,1)S(1)} async-done(((bf16[2,64,256]{2,0,1:T(2,128)(2,1)}), bf16[2,64,256]{2,0,1:T(2,128)(2,1)S(1)}, u32[]{:S(2)}, u32[]{:S(2)}) %all-to-all-start) | async-done | bytes 65568 | tf_op jit(solution)/shard_map/all_to_all | solution.py:58
  196.3 98.6 %all-reduce.1 = (f32[32,32]{0,1:T(8,128)S(1)}, f32[32,32]{0,1:T(8,128)S(1)}) all-reduce(f32[32,32]{0,1:T(8,128)S(1)} %convolution_bitcast_fusion.3, f32[32,32]{0,1:T(8,128)S(1)} %convolution_bitcast_fusion.2), channel_id=1, replica_groups=mesh['member'=16,'dp'=32] {'member','dp'}, use_global_device_ids=true, to_apply=%region_3.4 | all-reduce | flops 2048 | bytes 16384 | tf_op jit(solution)/shard_map/psum | solution.py:72
  294.9 2.9 cholesky.44
  297.9 0.6 compare_reduce_fusion.1
  298.5 0.7 fusion.42
  299.2 2.4 custom-call.11
  302.1 3.0 fusion.64
  305.2 2.2 all-gather.19.cloned.1.call-done
  307.4 3.0 fusion.65
  310.4 24.5 %all-gather.3 = f32[16,2,64]{2,1,0:T(2,128)S(1)} all-gather(f32[1,2,64]{2,1,0:T(2,128)S(1)} %bitcast.235), channel_id=1, replica_groups=mesh['member'=16,'dp'=32] {'member'}, dimensions={0}, use_global_device_ids=true | all-gather | bytes 8704 | tf_op jit(solution)/shard_map/all_gather | solution.py:78
  334.9 22.7 %all-gather.2 = f32[16,2,128]{2,1,0:T(2,128)S(1)} all-gather(f32[1,2,128]{2,1,0:T(2,128)S(1)} %bitcast.237), channel_id=1, replica_groups=mesh['member'=16,'dp'=32] {'member'}, dimensions={0}, use_global_device_ids=true | all-gather | bytes 17408 | tf_op jit(solution)/shard_map/all_gather | solution.py:76
  357.6 0.6 copy.102
  358.5 67.2 %all-gather.1 = bf16[2,4096]{1,0:T(2,128)(2,1)S(1)} all-gather(bf16[2,128]{1,0:T(2,128)(2,1)S(1)} %get-tuple-element.163), channel_id=3, replica_groups=mesh['member'=16,'dp'=32] {'dp'}, dimensions={1}, use_global_device_ids=true | all-gather | bytes 16896 | tf_op jit(solution)/shard_map/all_gather | solution.py:39
  425.8 1.8 copy.90
  427.7 32.0 %all-gather.25.cloned.1.call-done = bf16[2,64,4096]{2,0,1:T(2,128)(2,1)} async-done(((bf16[2,64,128]{2,0,1:T(2,128)(2,1)}), bf16[2,64,4096]{2,0,1:T(2,128)(2,1)}) %all-gather.25.cloned.1.call-update) | async-done | bytes 1048592 | tf_op jit(solution)/shard_map/all_gather | solution.py:37
  459.6 1.8 copy.91
  461.5 2.9 while.21
  461.5 1.4 fusion.96
  462.9 1.4 fusion.96
  464.4 0.7 copy.93
  465.1 7.3 %all-to-all-start.1 = ((bf16[2,64,256]{2,0,1:T(2,128)(2,1)}), bf16[2,64,256]{2,0,1:T(2,128)(2,1)S(1)}, u32[]{:S(2)}, u32[]{:S(2)}) async-start(bf16[2,64,256]{2,0,1:T(2,128)(2,1)} %copy.93), calls=%async_computation.1 | async-start | bytes 131072 | tf_op jit(solution)/shard_map/all_to_all | solution.py:58
  472.5 0.6 copy.100
  473.2 27.3 %all-gather.5 = f32[16,2,64]{2,1,0:T(2,128)S(1)} all-gather(f32[1,2,64]{2,1,0:T(2,128)S(1)} %bitcast.234), channel_id=1, replica_groups=mesh['member'=16,'dp'=32] {'member'}, dimensions={0}, use_global_device_ids=true | all-gather | bytes 8704 | tf_op jit(solution)/shard_map/all_gather | solution.py:78
  500.4 23.3 %all-gather.4 = f32[16,2,128]{2,1,0:T(2,128)S(1)} all-gather(f32[1,2,128]{2,1,0:T(2,128)S(1)} %bitcast.236), channel_id=1, replica_groups=mesh['member'=16,'dp'=32] {'member'}, dimensions={0}, use_global_device_ids=true | all-gather | bytes 17408 | tf_op jit(solution)/shard_map/all_gather | solution.py:76
  524.7 109.9 %all-reduce = (f32[32,32]{0,1:T(8,128)S(1)}, f32[32,32]{0,1:T(8,128)S(1)}) all-reduce(f32[32,32]{0,1:T(8,128)S(1)} %convolution_bitcast_fusion.1, f32[32,32]{0,1:T(8,128)S(1)} %convolution_bitcast_fusion), channel_id=1, replica_groups=mesh['member'=16,'dp'=32] {'member','dp'}, use_global_device_ids=true, to_apply=%region_10.14 | all-reduce | flops 2048 | bytes 16384 | tf_op jit(solution)/shard_map/psum | solution.py:72
  634.7 2.9 cholesky.55
  637.6 0.6 compare_reduce_fusion
  638.3 0.7 fusion.43
  638.9 2.4 custom-call.13
  641.9 2.4 convolution_add_fusion.2
  644.2 0.6 copy.105
  644.9 0.7 convolution_add_fusion.6
  645.6 0.7 convolution_add_fusion.7
  646.3 2.4 convolution_add_fusion.3
  648.7 0.6 copy.104
  (75 shorter events, 4.0 us)
Async XLA Ops:
  7.2 88.7 %all-gather.15.cloned.1.call-start = ((), (), s32[]{:S(2)}) async-start(), calls=%async_computation.2 | async-start | bytes 1081344 | tf_op jit(solution)/shard_map/all_gather | solution.py:38
  8.7 166.5 %all-gather.17.cloned.1.call-start = ((), (), s32[]{:S(2)}) async-start(), calls=%async_computation.3 | async-start | bytes 1081344 | tf_op jit(solution)/shard_map/all_gather | solution.py:37
  10.2 291.9 %all-gather.21.cloned.1.call-start = ((), (), s32[]{:S(2)}) async-start(), calls=%async_computation.5 | async-start | bytes 1114112 | tf_op jit(solution)/shard_map/all_gather | solution.py:77
  175.2 5.3 copy-start.4
  180.5 15.4 %copy-start.2 = (bf16[2,32,4,256]{3,2,1,0:T(4,128)(2,1)S(1)}, bf16[2,32,4,256]{3,2,1,0:T(4,128)(2,1)}, u32[]{:S(2)}) copy-start(bf16[2,32,4,256]{3,2,1,0:T(4,128)(2,1)} %param.18) | copy-start | bytes 393220
  180.5 15.4 %copy-start.3 = (f32[4,256]{1,0:T(4,128)S(1)}, f32[4,256]{1,0:T(4,128)}, u32[]{:S(2)}) copy-start(f32[4,256]{1,0:T(4,128)} %param.17) | copy-start | bytes 12292
  181.3 14.0 %all-to-all-start = ((bf16[2,64,256]{2,0,1:T(2,128)(2,1)}), bf16[2,64,256]{2,0,1:T(2,128)(2,1)S(1)}, u32[]{:S(2)}, u32[]{:S(2)}) async-start(bf16[2,64,256]{2,0,1:T(2,128)(2,1)} %copy.79), calls=%async_computation | async-start | bytes 131072 | tf_op jit(solution)/shard_map/all_to_all | solution.py:58
  187.9 119.4 %all-gather.19.cloned.1.call-start = ((), (), s32[]{:S(2)}) async-start(), calls=%async_computation.4 | async-start | bytes 1114112 | tf_op jit(solution)/shard_map/all_gather | solution.py:75
  188.5 237.3 %all-gather.23.cloned.1.call-start = ((), (), s32[]{:S(2)}) async-start(), calls=%async_computation.6 | async-start | bytes 1081344 | tf_op jit(solution)/shard_map/all_gather | solution.py:38
  195.4 106.7 %copy-start = (f32[2,64,128]{2,1,0:T(8,128)S(1)}, f32[2,64,128]{2,1,0:T(8,128)}, u32[]{:S(2)}) copy-start(f32[2,64,128]{2,1,0:T(8,128)} %param.21) | copy-start | bytes 196612
  196.0 111.4 %copy-start.1 = (f32[2,64,128]{2,1,0:T(8,128)S(1)}, f32[2,64,128]{2,1,0:T(8,128)}, u32[]{:S(2)}) copy-start(f32[2,64,128]{2,1,0:T(8,128)} %param.19) | copy-start | bytes 196612
  302.1 32.8 %copy-start.5 = (f32[2,128]{1,0:T(2,128)S(1)}, f32[2,128]{1,0:T(2,128)}, u32[]{:S(2)}) copy-start(f32[2,128]{1,0:T(2,128)} %param.20) | copy-start | bytes 3076
  305.1 154.5 %all-gather.25.cloned.1.call-start = ((), (), s32[]{:S(2)}) async-start(), calls=%async_computation.7 | async-start | bytes 1081344 | tf_op jit(solution)/shard_map/all_gather | solution.py:37
  310.4 331.5 %all-gather.29.cloned.1.call-start = ((), (), s32[]{:S(2)}) async-start(), calls=%async_computation.9 | async-start | bytes 1114112 | tf_op jit(solution)/shard_map/all_gather | solution.py:77
  427.6 33.8 %copy-start.6 = (bf16[256,64]{0,1:T(8,128)(2,1)S(1)}, bf16[256,64]{0,1:T(8,128)(2,1)}, u32[]{:S(2)}) copy-start(bf16[256,64]{0,1:T(8,128)(2,1)} %get-tuple-element.315) | copy-start | bytes 98308
  465.1 58.6 %all-to-all-start.1 = ((bf16[2,64,256]{2,0,1:T(2,128)(2,1)}), bf16[2,64,256]{2,0,1:T(2,128)(2,1)S(1)}, u32[]{:S(2)}, u32[]{:S(2)}) async-start(bf16[2,64,256]{2,0,1:T(2,128)(2,1)} %copy.93), calls=%async_computation.1 | async-start | bytes 131072 | tf_op jit(solution)/shard_map/all_to_all | solution.py:58
  472.4 173.9 %all-gather.27.cloned.1.call-start = ((), (), s32[]{:S(2)}) async-start(), calls=%async_computation.8 | async-start | bytes 1114112 | tf_op jit(solution)/shard_map/all_gather | solution.py:75
Sparse Core Ops, SparseCore 0:
  11.7 84.0 all-gather.14
  99.5 75.6 all-gather.16
  177.3 58.8 all-gather.20
  238.1 69.2 all-gather.18
  310.9 76.3 all-gather.22
  390.8 68.7 all-gather.24
  461.7 62.1 all-gather.28
  526.5 68.6 all-gather.26
where the time goes:
time: 657 us; the launch traced here: 656 us
  blocking collectives  422 us (64%)
  waiting for transfers between devices  157 us (24%)
  matrix products  22.2 us (3%)
  other arithmetic  17.7 us (3%)
  between operations  14.5 us (2%)
  starting transfers between devices  14.2 us (2%)
  local copies, waits for them, and re-layouts  8.08 us (1%)
    psum x2, blocking collectives, on_device(): gram, cross = lax.psum((gram_part, cross_part), ('member', 'dp'))  208 us
    all_gather x2, blocking collectives, predict(): lax.all_gather(shards[2], 'dp', axis=2, tiled=True)  116 us
    all_gather x2, waiting for transfers between devices, predict(): lax.all_gather(shards[0], 'dp', axis=2, tiled=True)  111 us
    all_gather x2, blocking collectives, on_device(): lax.all_gather(b_out, 'member', axis=0, tiled=True)  51.8 us
    all_gather x2, blocking collectives, on_device(): lax.all_gather(b_in, 'member', axis=0, tiled=True)  46 us
    all_gather x2, waiting for transfers between devices, predict(): lax.all_gather(shards[1], 'dp', axis=2, tiled=True)  35.2 us
    all_to_all x2, starting transfers between devices, on_device(): lax.all_to_all(predicted.astype(jnp.bfloat16), 'member', split_axis=1, co...  13.8 us
  transfers between devices with their start and end apart: 10, of which 5 were waited for; matrix products, arithmetic and copies ran while one was open for 7% of the time, Pallas kernels for 0%

commit v1 on v0

--- a/solution.py
+++ b/solution.py
@@ -36,7 +36,9 @@
         (
             lax.all_gather(shards[0], "dp", axis=2, tiled=True),
             lax.all_gather(shards[1], "dp", axis=2, tiled=True),
-            lax.all_gather(shards[2], "dp", axis=2, tiled=True),
+            jnp.concatenate(
+                lax.all_to_all(jnp.stack([shards[2]] * lax.axis_size("dp")), "dp", 0, 0), axis=2
+            ),
         ),
     )
     return total + b_out[:, :, None]

time: 657 us -> 657 us (level)
  blocking collectives: 422 us -> 306 us
  waiting for transfers between devices: 157 us -> 223 us
  starting transfers between devices: 14.2 us -> 63.5 us
    all_gather x2 -> x0, blocking collectives: 116 us -> none  [predict(): lax.all_gather(shards[2], 'dp', axis=2, tiled=True)]
    all_to_all x0 -> x2, starting transfers between devices: none -> 49.3 us  [predict(): lax.all_to_all(jnp.stack([shards[2]] * lax.axis_size('dp')), 'dp', 0, 0)]
    all_gather x2, waiting for transfers between devices: 111 us -> 143 us  [predict(): lax.all_gather(shards[0], 'dp', axis=2, tiled=True)]
    all_gather x2, waiting for transfers between devices: 35.2 us -> 59.8 us  [predict(): lax.all_gather(shards[1], 'dp', axis=2, tiled=True)]
    all_to_all x0 -> x2, waiting for transfers between devices: none -> 9.36 us  [predict(): lax.all_to_all(jnp.stack([shards[2]] * lax.axis_size('dp')), 'dp', 0, 0)]
  transfers between devices with their start and end apart: 10 -> 12, of which waited for: 5 -> 6; matrix products, arithmetic and copies ran while one was open for 7% -> 7% of each run, Pallas kernels for 0% -> 0%
where the time goes in v1:
time: 657 us; the launch traced here: 656 us
  blocking collectives  306 us (47%)
  waiting for transfers between devices  223 us (34%)
  starting transfers between devices  63.5 us (10%)
  matrix products  22.2 us (3%)
  other arithmetic  17.7 us (3%)
  between operations  14.5 us (2%)
  local copies, waits for them, and re-layouts  9.29 us (1%)
    psum x2, blocking collectives, on_device(): gram, cross = lax.psum((gram_part, cross_part), ('member', 'dp'))  207 us
    all_gather x2, waiting for transfers between devices, predict(): lax.all_gather(shards[0], 'dp', axis=2, tiled=True)  143 us
    all_gather x2, waiting for transfers between devices, predict(): lax.all_gather(shards[1], 'dp', axis=2, tiled=True)  59.8 us
    all_gather x2, blocking collectives, on_device(): lax.all_gather(b_out, 'member', axis=0, tiled=True)  51.9 us
    all_to_all x2, starting transfers between devices, predict(): lax.all_to_all(jnp.stack([shards[2]] * lax.axis_size('dp')), 'dp', 0, 0)  49.3 us
    all_gather x2, blocking collectives, on_device(): lax.all_gather(b_in, 'member', axis=0, tiled=True)  46.9 us
    all_to_all x2, starting transfers between devices, on_device(): lax.all_to_all(predicted.astype(jnp.bfloat16), 'member', split_axis=1, co...  13.8 us
  transfers between devices with their start and end apart: 12, of which 6 were waited for; matrix products, arithmetic and copies ran while one was open for 7% of the time, Pallas kernels for 0%

profile of v1, /device:TPU:1, one launch (start us, length us, event | category | flops | bytes accessed | tf_op | source)
XLA Modules:
  0.0 656.0 jit_solution(5785491708035342888)
XLA Ops:
  7.2 1.5 convert_element_type.118
  8.7 1.5 convert_element_type.119
  10.3 0.7 all-gather.19.cloned.1.call-update
  11.0 0.7 convert_element_type.120
  12.3 14.4 %all-to-all-start = ((bf16[32,2,1,128]{3,1,2,0:T(2,128)(2,1)}), bf16[32,2,1,128]{3,1,2,0:T(2,128)(2,1)S(1)}, u32[]{:S(2)}, u32[]{:S(2)}) async-start(bf16[32,2,1,128]{3,1,2,0:T(2,128)(2,1)} %stack.6), calls=%async_computation | async-start | bytes 32768 | tf_op jit(solution)/shard_map/all_to_all | solution.py:40
  26.7 9.4 %all-to-all-done = bf16[32,2,1,128]{3,1,2,0:T(2,128)(2,1)S(1)} async-done(((bf16[32,2,1,128]{3,1,2,0:T(2,128)(2,1)}), bf16[32,2,1,128]{3,1,2,0:T(2,128)(2,1)S(1)}, u32[]{:S(2)}, u32[]{:S(2)}) %all-to-all-start) | async-done | bytes 16416 | tf_op jit(solution)/shard_map/all_to_all | solution.py:40
  36.1 59.8 %all-gather.13.cloned.1.call-done = bf16[2,64,4096]{2,1,0:T(8,128)(2,1)} async-done(((bf16[2,64,128]{2,1,0:T(8,128)(2,1)}), bf16[2,64,4096]{2,1,0:T(8,128)(2,1)}) %all-gather.13.cloned.1.call-update) | async-done | bytes 1048592 | tf_op jit(solution)/shard_map/all_gather | solution.py:38
  95.8 79.4 %all-gather.15.cloned.1.call-done = bf16[2,64,4096]{2,1,0:T(8,128)(2,1)} async-done(((bf16[2,64,128]{2,1,0:T(8,128)(2,1)}), bf16[2,64,4096]{2,1,0:T(8,128)(2,1)}) %all-gather.15.cloned.1.call-update) | async-done | bytes 1048592 | tf_op jit(solution)/shard_map/all_gather | solution.py:37
  175.2 5.3 while.20
  175.3 2.6 fusion.92
  177.9 2.6 fusion.92
  180.6 0.7 copy.78
  181.3 6.6 %all-to-all-start.1 = ((bf16[2,64,256]{2,0,1:T(2,128)(2,1)}), bf16[2,64,256]{2,0,1:T(2,128)(2,1)S(1)}, u32[]{:S(2)}, u32[]{:S(2)}) async-start(bf16[2,64,256]{2,0,1:T(2,128)(2,1)} %copy.78), calls=%async_computation.1 | async-start | bytes 131072 | tf_op jit(solution)/shard_map/all_to_all | solution.py:60
  188.5 6.8 %all-to-all-done.1 = bf16[2,64,256]{2,0,1:T(2,128)(2,1)S(1)} async-done(((bf16[2,64,256]{2,0,1:T(2,128)(2,1)}), bf16[2,64,256]{2,0,1:T(2,128)(2,1)S(1)}, u32[]{:S(2)}, u32[]{:S(2)}) %all-to-all-start.1) | async-done | bytes 65568 | tf_op jit(solution)/shard_map/all_to_all | solution.py:60
  196.3 98.5 %all-reduce.1 = (f32[32,32]{0,1:T(8,128)S(1)}, f32[32,32]{0,1:T(8,128)S(1)}) all-reduce(f32[32,32]{0,1:T(8,128)S(1)} %convolution_bitcast_fusion.3, f32[32,32]{0,1:T(8,128)S(1)} %convolution_bitcast_fusion.2), channel_id=1, replica_groups=mesh['member'=16,'dp'=32] {'member','dp'}, use_global_device_ids=true, to_apply=%region_3.4 | all-reduce | flops 2048 | bytes 16384 | tf_op jit(solution)/shard_map/psum | solution.py:74
  294.9 2.9 cholesky.44
  297.8 0.6 compare_reduce_fusion.1
  298.5 0.7 fusion.42
  299.1 2.4 custom-call.11
  302.1 3.0 fusion.64
  305.2 2.2 all-gather.17.cloned.1.call-done
  307.3 3.0 fusion.65
  310.4 24.7 %all-gather.1 = f32[16,2,64]{2,1,0:T(2,128)S(1)} all-gather(f32[1,2,64]{2,1,0:T(2,128)S(1)} %bitcast.239), channel_id=1, replica_groups=mesh['member'=16,'dp'=32] {'member'}, dimensions={0}, use_global_device_ids=true | all-gather | bytes 8704 | tf_op jit(solution)/shard_map/all_gather | solution.py:80
  335.1 22.7 %all-gather = f32[16,2,128]{2,1,0:T(2,128)S(1)} all-gather(f32[1,2,128]{2,1,0:T(2,128)S(1)} %bitcast.241), channel_id=1, replica_groups=mesh['member'=16,'dp'=32] {'member'}, dimensions={0}, use_global_device_ids=true | all-gather | bytes 17408 | tf_op jit(solution)/shard_map/all_gather | solution.py:78
  357.7 0.6 copy.101
  359.1 34.9 %all-to-all-start.2 = ((bf16[32,2,1,128]{3,1,2,0:T(2,128)(2,1)}), bf16[32,2,1,128]{3,1,2,0:T(2,128)(2,1)S(1)}, u32[]{:S(2)}, u32[]{:S(2)}) async-start(bf16[32,2,1,128]{3,1,2,0:T(2,128)(2,1)} %stack.7), calls=%async_computation.2 | async-start | bytes 32768 | tf_op jit(solution)/shard_map/all_to_all | solution.py:40
  394.1 1.8 copy.89
  396.0 63.8 %all-gather.23.cloned.1.call-done = bf16[2,64,4096]{2,0,1:T(2,128)(2,1)} async-done(((bf16[2,64,128]{2,0,1:T(2,128)(2,1)}), bf16[2,64,4096]{2,0,1:T(2,128)(2,1)}) %all-gather.23.cloned.1.call-update) | async-done | bytes 1048592 | tf_op jit(solution)/shard_map/all_gather | solution.py:37
  459.8 1.8 copy.90
  461.6 2.9 while.21
  461.6 1.4 fusion.96
  463.1 1.4 fusion.96
  464.6 0.7 copy.92
  465.3 7.3 %all-to-all-start.3 = ((bf16[2,64,256]{2,0,1:T(2,128)(2,1)}), bf16[2,64,256]{2,0,1:T(2,128)(2,1)S(1)}, u32[]{:S(2)}, u32[]{:S(2)}) async-start(bf16[2,64,256]{2,0,1:T(2,128)(2,1)} %copy.92), calls=%async_computation.3 | async-start | bytes 131072 | tf_op jit(solution)/shard_map/all_to_all | solution.py:60
  472.6 0.6 copy.99
  473.3 27.3 %all-gather.3 = f32[16,2,64]{2,1,0:T(2,128)S(1)} all-gather(f32[1,2,64]{2,1,0:T(2,128)S(1)} %bitcast.238), channel_id=1, replica_groups=mesh['member'=16,'dp'=32] {'member'}, dimensions={0}, use_global_device_ids=true | all-gather | bytes 8704 | tf_op jit(solution)/shard_map/all_gather | solution.py:80
  500.6 24.3 %all-gather.2 = f32[16,2,128]{2,1,0:T(2,128)S(1)} all-gather(f32[1,2,128]{2,1,0:T(2,128)S(1)} %bitcast.240), channel_id=1, replica_groups=mesh['member'=16,'dp'=32] {'member'}, dimensions={0}, use_global_device_ids=true | all-gather | bytes 17408 | tf_op jit(solution)/shard_map/all_gather | solution.py:78
  525.8 108.7 %all-reduce = (f32[32,32]{0,1:T(8,128)S(1)}, f32[32,32]{0,1:T(8,128)S(1)}) all-reduce(f32[32,32]{0,1:T(8,128)S(1)} %convolution_bitcast_fusion.1, f32[32,32]{0,1:T(8,128)S(1)} %convolution_bitcast_fusion), channel_id=1, replica_groups=mesh['member'=16,'dp'=32] {'member','dp'}, use_global_device_ids=true, to_apply=%region_10.14 | all-reduce | flops 2048 | bytes 16384 | tf_op jit(solution)/shard_map/psum | solution.py:74
  634.6 2.9 cholesky.55
  637.5 0.6 compare_reduce_fusion
  638.1 0.7 fusion.43
  638.8 2.4 custom-call.13
  641.7 2.4 convolution_add_fusion.2
  644.1 0.6 copy.104
  644.7 0.7 convolution_add_fusion.6
  645.4 0.7 convolution_add_fusion.7
  646.1 2.4 convolution_add_fusion.3
  648.5 0.6 copy.103
  (79 shorter events, 5.7 us)
Async XLA Ops:
  7.2 88.7 %all-gather.13.cloned.1.call-start = ((), (), s32[]{:S(2)}) async-start(), calls=%async_computation.4 | async-start | bytes 1081344 | tf_op jit(solution)/shard_map/all_gather | solution.py:38
  8.7 166.5 %all-gather.15.cloned.1.call-start = ((), (), s32[]{:S(2)}) async-start(), calls=%async_computation.5 | async-start | bytes 1081344 | tf_op jit(solution)/shard_map/all_gather | solution.py:37
  10.2 291.8 %all-gather.19.cloned.1.call-start = ((), (), s32[]{:S(2)}) async-start(), calls=%async_computation.7 | async-start | bytes 1114112 | tf_op jit(solution)/shard_map/all_gather | solution.py:79
  12.3 23.8 %all-to-all-start = ((bf16[32,2,1,128]{3,1,2,0:T(2,128)(2,1)}), bf16[32,2,1,128]{3,1,2,0:T(2,128)(2,1)S(1)}, u32[]{:S(2)}, u32[]{:S(2)}) async-start(bf16[32,2,1,128]{3,1,2,0:T(2,128)(2,1)} %stack.6), calls=%async_computation | async-start | bytes 32768 | tf_op jit(solution)/shard_map/all_to_all | solution.py:40
  175.2 5.3 copy-start.4
  180.5 15.4 %copy-start.2 = (bf16[2,32,4,256]{3,2,1,0:T(4,128)(2,1)S(1)}, bf16[2,32,4,256]{3,2,1,0:T(4,128)(2,1)}, u32[]{:S(2)}) copy-start(bf16[2,32,4,256]{3,2,1,0:T(4,128)(2,1)} %param.18) | copy-start | bytes 393220
  180.5 15.4 %copy-start.3 = (f32[4,256]{1,0:T(4,128)S(1)}, f32[4,256]{1,0:T(4,128)}, u32[]{:S(2)}) copy-start(f32[4,256]{1,0:T(4,128)} %param.17) | copy-start | bytes 12292
  181.3 14.0 %all-to-all-start.1 = ((bf16[2,64,256]{2,0,1:T(2,128)(2,1)}), bf16[2,64,256]{2,0,1:T(2,128)(2,1)S(1)}, u32[]{:S(2)}, u32[]{:S(2)}) async-start(bf16[2,64,256]{2,0,1:T(2,128)(2,1)} %copy.78), calls=%async_computation.1 | async-start | bytes 131072 | tf_op jit(solution)/shard_map/all_to_all | solution.py:60
  187.9 119.4 %all-gather.17.cloned.1.call-start = ((), (), s32[]{:S(2)}) async-start(), calls=%async_computation.6 | async-start | bytes 1114112 | tf_op jit(solution)/shard_map/all_gather | solution.py:77
  188.5 205.7 %all-gather.21.cloned.1.call-start = ((), (), s32[]{:S(2)}) async-start(), calls=%async_computation.8 | async-start | bytes 1081344 | tf_op jit(solution)/shard_map/all_gather | solution.py:38
  195.4 106.6 %copy-start = (f32[2,64,128]{2,1,0:T(8,128)S(1)}, f32[2,64,128]{2,1,0:T(8,128)}, u32[]{:S(2)}) copy-start(f32[2,64,128]{2,1,0:T(8,128)} %param.21) | copy-start | bytes 196612
  195.9 111.4 %copy-start.1 = (f32[2,64,128]{2,1,0:T(8,128)S(1)}, f32[2,64,128]{2,1,0:T(8,128)}, u32[]{:S(2)}) copy-start(f32[2,64,128]{2,1,0:T(8,128)} %param.19) | copy-start | bytes 196612
  302.1 33.0 %copy-start.5 = (f32[2,128]{1,0:T(2,128)S(1)}, f32[2,128]{1,0:T(2,128)}, u32[]{:S(2)}) copy-start(f32[2,128]{1,0:T(2,128)} %param.20) | copy-start | bytes 3076
  305.1 154.7 %all-gather.23.cloned.1.call-start = ((), (), s32[]{:S(2)}) async-start(), calls=%async_computation.9 | async-start | bytes 1081344 | tf_op jit(solution)/shard_map/all_gather | solution.py:37
  310.3 331.4 %all-gather.27.cloned.1.call-start = ((), (), s32[]{:S(2)}) async-start(), calls=%async_computation.11 | async-start | bytes 1114112 | tf_op jit(solution)/shard_map/all_gather | solution.py:79
  359.1 102.4 %all-to-all-start.2 = ((bf16[32,2,1,128]{3,1,2,0:T(2,128)(2,1)}), bf16[32,2,1,128]{3,1,2,0:T(2,128)(2,1)S(1)}, u32[]{:S(2)}, u32[]{:S(2)}) async-start(bf16[32,2,1,128]{3,1,2,0:T(2,128)(2,1)} %stack.7), calls=%async_computation.2 | async-start | bytes 32768 | tf_op jit(solution)/shard_map/all_to_all | solution.py:40
  396.0 65.6 %copy-start.6 = (bf16[256,64]{0,1:T(8,128)(2,1)S(1)}, bf16[256,64]{0,1:T(8,128)(2,1)}, u32[]{:S(2)}) copy-start(bf16[256,64]{0,1:T(8,128)(2,1)} %get-tuple-element.317) | copy-start | bytes 98308
  465.3 59.6 %all-to-all-start.3 = ((bf16[2,64,256]{2,0,1:T(2,128)(2,1)}), bf16[2,64,256]{2,0,1:T(2,128)(2,1)S(1)}, u32[]{:S(2)}, u32[]{:S(2)}) async-start(bf16[2,64,256]{2,0,1:T(2,128)(2,1)} %copy.92), calls=%async_computation.3 | async-start | bytes 131072 | tf_op jit(solution)/shard_map/all_to_all | solution.py:60
  472.5 173.6 %all-gather.25.cloned.1.call-start = ((), (), s32[]{:S(2)}) async-start(), calls=%async_computation.10 | async-start | bytes 1114112 | tf_op jit(solution)/shard_map/all_gather | solution.py:77
Sparse Core Ops, SparseCore 0:
  11.7 84.0 all-gather.12
  99.5 75.6 all-gather.14
  177.3 58.8 all-gather.18
  238.1 69.1 all-gather.16
  310.8 76.3 all-gather.20
  390.8 68.8 all-gather.22
  461.8 61.3 all-gather.26
  525.8 69.5 all-gather.24
